TPU v7x, 128 devices: a whole 4x4x4 slice. The times are simulated.
128 devices in a mesh: slab: 32 (over x, y, core), pencil: 4 (over z).
Axes of the slice: x: 4, y: 4, z: 4, core: 2. Of those that a mesh axis runs over, the one named last changes fastest.
Arguments:
- cotangent: float32 [128, 512, 512], P('slab', 'pencil'), may hold values from -6 to 6
- seg_rows: int32 [32, 4], replicated, may hold values from 1 to 64, 128 in all within a row
- owners: int32 [32, 4], replicated, may hold values from 0 to 127
- offsets: int32 [32, 4], replicated, may hold values from 0 to 64
Outputs:
- rhs_grad: float32 [128, 512, 512], P('slab', 'pencil')
- parent_grad: float32 [128, 128, 128], P(('slab', 'pencil'))
Inputs may be any that keep to these rules, and one draw needn't show every extreme that they name: `seg_rows`: each tile's 4 row counts sum to 128; in every tile one segment has exactly 64 rows.
All inputs are finite; a program needn't handle non-finite values.
Results may differ from a plain program's by a relative error of at most 0.00002.
Values sent between devices are 32-bit elements; how exact they have to be, the bound alone decides.
No kernel may reach another device: no remote copies, remote signals or barrier semaphores. Data moves between devices by JAX's collectives and lax.ppermute only.
A program may use at most 192 MiB of HBM per device.

v0:
```python
import jax
import jax.numpy as jnp
from jax import lax
from jax.sharding import PartitionSpec as P

TILE = 128
PT_DEV = 1
omega_weight = 2.0 / 3.0


def with_halo(x, sides, width):
    for axis, dim in sides:
        peers, length = (lax.axis_size(axis), x.shape[dim])
        up = [(i, (i + 1) % peers) for i in range(peers - 1)]
        down = [(j, i) for i, j in up]
        last = lax.slice_in_dim(x, length - width, length, axis=dim)
        initial = lax.slice_in_dim(x, 0, width, axis=dim)
        before = lax.ppermute(last, axis, up)
        after = lax.ppermute(initial, axis, down)
        x = jnp.concatenate([before, x, after], axis=dim)
    return x


def neighbour_sum(padded):
    total = padded[2:, 1:-1, 1:-1] + padded[:-2, 1:-1, 1:-1]
    total = total + padded[1:-1, 2:, 1:-1] + padded[1:-1, :-2, 1:-1]
    total = total + padded[1:-1, 1:-1, 2:] + padded[1:-1, 1:-1, :-2]
    return total


def block_neighbours(field):
    padded = with_halo(field, (("slab", 0), ("pencil", 1)), 1)
    return neighbour_sum(jnp.pad(padded, ((0, 0), (0, 0), (1, 1))))


def coarse_neighbours(field):
    padded = with_halo(field, (("slab", 0), ("pencil", 1)), 1)
    return neighbour_sum(jnp.pad(padded, ((0, 0), (0, 0), (1, 1))))


def coefficient(level):
    return omega_weight * 4.0**level / 6.0


def smoothed(field, neighbours):
    return (1.0 - omega_weight) * field + omega_weight / 6.0 * neighbours


def children_sum(field):
    x_cells, y_cells, z_cells = field.shape
    blocks = field.reshape(x_cells // 2, 2, y_cells // 2, 2, z_cells // 2, 2)
    return jnp.sum(blocks, axis=(1, 3, 5))


def prolong(field):
    return jnp.repeat(jnp.repeat(jnp.repeat(field, 2, axis=0), 2, axis=1), 2, axis=2)


def source_rows(seg_rows, owners, offsets, tile_size):
    starts = jnp.cumsum(seg_rows, axis=1) - seg_rows
    position = jnp.arange(tile_size, dtype=jnp.int32)[None, None, :]
    inside = (position >= starts[:, :, None]) & (position < (starts + seg_rows)[:, :, None])
    value = owners[:, :, None] * tile_size + offsets[:, :, None] + position - starts[:, :, None]
    return jnp.sum(jnp.where(inside, value, 0), axis=1)


def tile_rows(faces, tile_size):
    face_count, y_cells, z_cells = faces.shape
    blocks = faces.reshape(
        face_count, y_cells // tile_size, tile_size, z_cells // tile_size, tile_size
    )
    return blocks.transpose(0, 1, 3, 2, 4).reshape(-1, tile_size)


def add_rows(rows_data, targets, first_row, slot_count):
    shifted = targets - first_row
    segment_ids = jnp.where((shifted >= 0) & (shifted < slot_count), shifted, slot_count)
    summed = jax.ops.segment_sum(rows_data, segment_ids, num_segments=slot_count + 1)
    return summed[:slot_count]


def shards(cotangent, seg_rows, owners, offsets):
    x_cells, y_cells, z_cells = cotangent.shape
    tile_size = TILE
    grad_fine = cotangent
    rhs_grad = jnp.zeros_like(cotangent)
    for sweep_number in range(3):
        rhs_grad = rhs_grad + coefficient(0) * grad_fine
        grad_fine = smoothed(grad_fine, block_neighbours(grad_fine))
    medium = children_sum(grad_fine)
    grad_medium = jnp.zeros_like(medium)
    for sweep_number in range(3):
        grad_medium = grad_medium + coefficient(1) * medium
        medium = smoothed(medium, block_neighbours(medium))
    coarse_cot = children_sum(medium)
    grad_coarse = coefficient(2) * coarse_cot
    for sweep_number in range(2):
        coarse_cot = smoothed(coarse_cot, coarse_neighbours(coarse_cot))
        grad_coarse = grad_coarse + coefficient(2) * coarse_cot
    back_medium = prolong(grad_coarse) * 0.125
    grad_medium = grad_medium + back_medium
    medium = medium - (6.0 * back_medium - block_neighbours(back_medium)) / 4.0
    for sweep_number in range(3):
        grad_medium = grad_medium + coefficient(1) * medium
        if sweep_number < 2:
            medium = smoothed(medium, block_neighbours(medium))
    back_fine = prolong(grad_medium) * 0.125
    rhs_grad = rhs_grad + back_fine
    grad_fine = grad_fine - (6.0 * back_fine - block_neighbours(back_fine))
    for sweep_number in range(3):
        rhs_grad = rhs_grad + coefficient(0) * grad_fine
        if sweep_number < 2:
            grad_fine = smoothed(grad_fine, block_neighbours(grad_fine))
    slab_index = lax.axis_index("slab")
    slab_count = lax.axis_size("slab")
    low_part = jnp.where(slab_index == 0, rhs_grad[0], 0.0)
    high_part = jnp.where(slab_index == slab_count - 1, rhs_grad[x_cells - 1], 0.0)
    summed_faces = lax.psum(jnp.stack([low_part, high_part]), "slab")
    all_faces = lax.all_gather(summed_faces, "pencil", axis=1, tiled=True)
    all_rows = tile_rows(all_faces, tile_size)
    targets = source_rows(seg_rows, owners, offsets, tile_size)
    first_row = lax.axis_index(("slab", "pencil")) * (PT_DEV * tile_size)
    owned = add_rows(all_rows, targets.reshape(-1), first_row, PT_DEV * tile_size)
    parent_grad = owned.reshape(PT_DEV, tile_size, tile_size)
    return (rhs_grad, parent_grad)


def solution(mesh):
    return jax.shard_map(
        shards,
        mesh=mesh,
        in_specs=(P("slab", "pencil", None), P(), P(), P()),
        out_specs=(P("slab", "pencil", None), P(("slab", "pencil"), None, None)),
        check_vma=False,
    )
```

profile of v0, /device:TPU:0, one launch (start us, length us, event | category | flops | bytes accessed | tf_op | source)
XLA Modules:
  0.0 669.0 jit_solution(12144026256965964843)
XLA Ops:
  10.1 3.0 collective-permute-start.1
  21.6 4.6 collective-permute-start.3
  29.2 3.6 select_maximum_fusion.20
  32.8 2.7 fusion.29
  36.8 5.0 collective-permute-start.5
  50.3 4.5 collective-permute-start.7
  58.3 3.3 select_maximum_fusion.16
  61.6 2.4 fusion.24
  65.4 8.1 %collective-permute-start.9 = (f32[1,128,512]{1,2,0:T(8,128)S(1)}, f32[1,128,512]{1,2,0:T(8,128)S(1)}, u32[]{:S(2)}, u32[]{:S(2)}) collective-permute-start(f32[1,128,512]{1,2,0:T(8,128)S(1)} %get-tuple-element.34), channel_id=1, source_target_pairs={{0,4},{4,8},{8,12},{12,16},{16,20},{20,24},{24,28},{28,32},{32,36}... | collective-permute-start | bytes 786440 | tf_op jit(solution)/shard_map/ppermute | solution.py:18
  82.7 5.0 collective-permute-start.11
  91.0 3.3 select_maximum_fusion.12
  94.4 2.4 fusion.19
  96.8 2.6 copy.138
  99.4 69.2 %reshape.120 = f32[2,2,64,2,256,2]{5,4,3,2,1,0:T(8,128)} reshape(f32[4,128,512]{2,1,0:T(8,128)} %copy.138) | data formatting | bytes 2097152 | tf_op jit(solution)/shard_map/reshape | solution.py:51
  168.6 20.8 %reduce_sum.36 = f32[2,64,256]{2,1,0:T(8,128)S(1)} reduce(f32[2,2,64,2,256,2]{5,4,3,2,1,0:T(8,128)} %reshape.120, f32[]{:T(128)} %constant.17.clone.1), dimensions={1,3,5}, to_apply=%region_0.1 | reduce | flops 229376 | bytes 1179652 | tf_op jit(solution)/shard_map/reduce_sum | solution.py:52
  190.7 7.2 %collective-permute-start.13 = (f32[1,64,256]{2,1,0:T(8,128)S(1)}, f32[1,64,256]{2,1,0:T(8,128)S(1)}, u32[]{:S(2)}, u32[]{:S(2)}) collective-permute-start(f32[1,64,256]{2,1,0:T(8,128)S(1)} %get-tuple-element.62), channel_id=1, source_target_pairs={{0,4},{4,8},{8,12},{12,16},{16,20},{20,24},{24,28},{28,32},{32,36}... | collective-permute-start | bytes 196616 | tf_op jit(solution)/shard_map/ppermute | solution.py:18
  200.0 4.5 collective-permute-start.15
  207.5 4.9 collective-permute-start.17
  214.6 4.5 collective-permute-start.19
  222.1 5.6 collective-permute-start.21
  229.9 4.5 collective-permute-start.23
  237.4 6.3 reduce_sum.38
  243.7 2.8 reduce_sum.39
  247.8 5.6 collective-permute-start.25
  255.5 4.5 collective-permute-start.27
  262.8 5.2 collective-permute-start.29
  270.1 4.5 collective-permute-start.31
  281.7 5.8 collective-permute-start.33
  295.9 4.5 collective-permute-start.35
  310.2 5.0 collective-permute-start.37
  317.4 4.6 collective-permute-start.39
  324.9 3.8 collective-permute-start.41
  330.9 4.7 collective-permute-start.43
  344.9 6.3 collective-permute-start.45
  363.3 2.5 copy.155
  365.7 5.1 collective-permute-start.47
  382.3 3.7 select_maximum_fusion.8
  386.4 2.4 fusion.14
  390.1 5.4 collective-permute-start.49
  404.7 4.8 collective-permute-start.51
  412.8 3.7 select_maximum_fusion.4
  419.3 9.8 %collective-permute-start.53 = (f32[1,128,512]{1,2,0:T(8,128)S(1)}, f32[1,128,512]{1,2,0:T(8,128)S(1)}, u32[]{:S(2)}, u32[]{:S(2)}) collective-permute-start(f32[1,128,512]{1,2,0:T(8,128)S(1)} %get-tuple-element.30), channel_id=1, source_target_pairs={{0,4},{4,8},{8,12},{12,16},{16,20},{20,24},{24,28},{28,32},{32,36}... | collective-permute-start | bytes 786440 | tf_op jit(solution)/shard_map/ppermute | solution.py:18
  438.2 4.8 collective-permute-start.55
  446.4 3.7 select_maximum_fusion
  454.5 138.5 %all-reduce.16.cloned.1.call-done = f32[2,128,512]{1,2,0:T(8,128)} async-done(((f32[2,128,512]{1,2,0:T(8,128)}), f32[2,128,512]{1,2,0:T(8,128)}) %all-reduce.16.cloned.1.call-update) | async-done | bytes 524304 | tf_op jit(solution)/shard_map/psum | solution.py:118
  593.2 2.5 copy.172
  595.8 32.8 %all-gather.2.cloned.1.call-done = f32[2,512,512]{1,2,0:T(8,128)} async-done(((f32[2,128,512]{1,2,0:T(8,128)}), f32[2,512,512]{1,2,0:T(8,128)}) %all-gather.2.cloned.1.call-update) | async-done | bytes 2097168 | tf_op jit(solution)/shard_map/all_gather | solution.py:119
  632.4 29.0 %scatter_custom_fusion = f32[129,128]{1,0:T(8,128)S(1)} fusion(s32[4096]{0:T(1024)S(1)} %bitcast.53, f32[4096,128]{1,0:T(8,128)} %bitcast.39, f32[]{:T(128)} %constant.17.clone.1), kind=kCustom, calls=%fused_computation.276 | custom fusion | flops 524288 | bytes 66560 | tf_op jit(solution)/shard_map/scatter-add | solution.py:78
  (278 shorter events, 169.3 us)
Async XLA Ops:
  7.2 585.8 %all-reduce.16.cloned.1.call-start = ((), (), s32[]{:S(2)}) async-start(), calls=%async_computation | async-start | bytes 1048576 | tf_op jit(solution)/shard_map/psum | solution.py:118
  18.4 7.7 %collective-permute-start.2 = (f32[6,1,512]{2,1,0:T(1,128)S(1)}, f32[6,1,512]{2,1,0:T(1,128)S(1)}, u32[]{:S(2)}, u32[]{:S(2)}) collective-permute-start(f32[6,1,512]{2,1,0:T(1,128)S(1)} %copy.119), channel_id=1, source_target_pairs={{1,0},{2,1},{3,2},{5,4},{6,5},{7,6},{9,8},{10,9},{11,10},{13,12},{... | collective-permute-start | bytes 36872 | tf_op jit(solution)/shard_map/ppermute | solution.py:19
  21.6 6.0 collective-permute-start.3
  35.5 6.4 collective-permute-start.4
  36.8 6.2 collective-permute-start.5
  47.2 7.7 %collective-permute-start.6 = (f32[6,1,512]{2,1,0:T(1,128)S(1)}, f32[6,1,512]{2,1,0:T(1,128)S(1)}, u32[]{:S(2)}, u32[]{:S(2)}) collective-permute-start(f32[6,1,512]{2,1,0:T(1,128)S(1)} %copy.126), channel_id=1, source_target_pairs={{1,0},{2,1},{3,2},{5,4},{6,5},{7,6},{9,8},{10,9},{11,10},{13,12},{... | collective-permute-start | bytes 36872 | tf_op jit(solution)/shard_map/ppermute | solution.py:19
  50.3 6.2 collective-permute-start.7
  64.1 9.4 %collective-permute-start.8 = (f32[1,128,512]{1,2,0:T(8,128)S(1)}, f32[1,128,512]{1,2,0:T(8,128)S(1)}, u32[]{:S(2)}, u32[]{:S(2)}) collective-permute-start(f32[1,128,512]{1,2,0:T(8,128)S(1)} %get-tuple-element.35), channel_id=1, source_target_pairs={{4,0},{8,4},{12,8},{16,12},{20,16},{24,20},{28,24},{32,28},{36,32}... | collective-permute-start | bytes 786440 | tf_op jit(solution)/shard_map/ppermute | solution.py:19
  65.4 9.3 %collective-permute-start.9 = (f32[1,128,512]{1,2,0:T(8,128)S(1)}, f32[1,128,512]{1,2,0:T(8,128)S(1)}, u32[]{:S(2)}, u32[]{:S(2)}) collective-permute-start(f32[1,128,512]{1,2,0:T(8,128)S(1)} %get-tuple-element.34), channel_id=1, source_target_pairs={{0,4},{4,8},{8,12},{12,16},{16,20},{20,24},{24,28},{28,32},{32,36}... | collective-permute-start | bytes 786440 | tf_op jit(solution)/shard_map/ppermute | solution.py:18
  79.5 8.2 %collective-permute-start.10 = (f32[6,1,512]{2,1,0:T(1,128)S(1)}, f32[6,1,512]{2,1,0:T(1,128)S(1)}, u32[]{:S(2)}, u32[]{:S(2)}) collective-permute-start(f32[6,1,512]{2,1,0:T(1,128)S(1)} %copy.132), channel_id=1, source_target_pairs={{1,0},{2,1},{3,2},{5,4},{6,5},{7,6},{9,8},{10,9},{11,10},{13,12},{... | collective-permute-start | bytes 36872 | tf_op jit(solution)/shard_map/ppermute | solution.py:19
  82.7 6.7 %collective-permute-start.11 = (f32[6,1,512]{2,1,0:T(1,128)S(1)}, f32[6,1,512]{2,1,0:T(1,128)S(1)}, u32[]{:S(2)}, u32[]{:S(2)}) collective-permute-start(f32[6,1,512]{2,1,0:T(1,128)S(1)} %copy.134), channel_id=1, source_target_pairs={{0,1},{1,2},{2,3},{4,5},{5,6},{6,7},{8,9},{9,10},{10,11},{12,13},{... | collective-permute-start | bytes 36872 | tf_op jit(solution)/shard_map/ppermute | solution.py:18
  189.4 8.5 %collective-permute-start.12 = (f32[1,64,256]{2,1,0:T(8,128)S(1)}, f32[1,64,256]{2,1,0:T(8,128)S(1)}, u32[]{:S(2)}, u32[]{:S(2)}) collective-permute-start(f32[1,64,256]{2,1,0:T(8,128)S(1)} %get-tuple-element.63), channel_id=1, source_target_pairs={{4,0},{8,4},{12,8},{16,12},{20,16},{24,20},{28,24},{32,28},{36,32}... | collective-permute-start | bytes 196616 | tf_op jit(solution)/shard_map/ppermute | solution.py:19
  190.7 8.1 %collective-permute-start.13 = (f32[1,64,256]{2,1,0:T(8,128)S(1)}, f32[1,64,256]{2,1,0:T(8,128)S(1)}, u32[]{:S(2)}, u32[]{:S(2)}) collective-permute-start(f32[1,64,256]{2,1,0:T(8,128)S(1)} %get-tuple-element.62), channel_id=1, source_target_pairs={{0,4},{4,8},{8,12},{12,16},{16,20},{20,24},{24,28},{28,32},{32,36}... | collective-permute-start | bytes 196616 | tf_op jit(solution)/shard_map/ppermute | solution.py:18
  198.7 5.8 collective-permute-start.14
  200.0 5.9 collective-permute-start.15
  206.2 6.2 collective-permute-start.16
  213.3 5.8 collective-permute-start.18
  214.6 5.9 collective-permute-start.19
  220.8 6.9 %collective-permute-start.20 = (f32[1,64,256]{2,1,0:T(8,128)S(1)}, f32[1,64,256]{2,1,0:T(8,128)S(1)}, u32[]{:S(2)}, u32[]{:S(2)}) collective-permute-start(f32[1,64,256]{2,1,0:T(8,128)S(1)} %get-tuple-element.59), channel_id=1, source_target_pairs={{4,0},{8,4},{12,8},{16,12},{20,16},{24,20},{28,24},{32,28},{36,32}... | collective-permute-start | bytes 196616 | tf_op jit(solution)/shard_map/ppermute | solution.py:19
  222.1 6.5 collective-permute-start.21
  229.9 5.9 collective-permute-start.23
  246.5 6.9 %collective-permute-start.24 = (f32[1,32,128]{2,1,0:T(8,128)S(1)}, f32[1,32,128]{2,1,0:T(8,128)S(1)}, u32[]{:S(2)}, u32[]{:S(2)}) collective-permute-start(f32[1,32,128]{2,1,0:T(8,128)S(1)} %bitcast.45), channel_id=1, source_target_pairs={{4,0},{8,4},{12,8},{16,12},{20,16},{24,20},{28,24},{32,28},{36,32}... | collective-permute-start | bytes 49160 | tf_op jit(solution)/shard_map/ppermute | solution.py:19
  247.8 6.4 collective-permute-start.25
  261.5 6.5 collective-permute-start.28
  262.8 6.0 collective-permute-start.29
  280.4 8.7 %collective-permute-start.32 = (f32[1,64,256]{1,2,0:T(8,128)}, f32[1,64,256]{1,2,0:T(8,128)}, u32[]{:S(2)}, u32[]{:S(2)}) collective-permute-start(f32[1,64,256]{1,2,0:T(8,128)} %bitcast.7), channel_id=1, source_target_pairs={{4,0},{8,4},{12,8},{16,12},{20,16},{24,20},{28,24},{32,28},{36,32}... | collective-permute-start | bytes 196616 | tf_op jit(solution)/shard_map/ppermute | solution.py:19
  281.7 9.0 %collective-permute-start.33 = (f32[1,64,256]{1,2,0:T(8,128)}, f32[1,64,256]{1,2,0:T(8,128)}, u32[]{:S(2)}, u32[]{:S(2)}) collective-permute-start(f32[1,64,256]{1,2,0:T(8,128)} %bitcast.7), channel_id=1, source_target_pairs={{0,4},{4,8},{8,12},{12,16},{16,20},{20,24},{24,28},{28,32},{32,36}... | collective-permute-start | bytes 196616 | tf_op jit(solution)/shard_map/ppermute | solution.py:18
  294.6 11.8 %collective-permute-start.34 = (f32[4,1,256]{2,1,0:T(1,128)S(1)}, f32[4,1,256]{2,1,0:T(1,128)S(1)}, u32[]{:S(2)}, u32[]{:S(2)}) collective-permute-start(f32[4,1,256]{2,1,0:T(1,128)S(1)} %get-tuple-element.47), channel_id=1, source_target_pairs={{1,0},{2,1},{3,2},{5,4},{6,5},{7,6},{9,8},{10,9},{11,10},{13,12},{... | collective-permute-start | bytes 12296 | tf_op jit(solution)/shard_map/ppermute | solution.py:19
  295.9 10.5 %collective-permute-start.35 = (f32[4,1,256]{2,1,0:T(1,128)S(1)}, f32[4,1,256]{2,1,0:T(1,128)S(1)}, u32[]{:S(2)}, u32[]{:S(2)}) collective-permute-start(f32[4,1,256]{2,1,0:T(1,128)S(1)} %get-tuple-element.46), channel_id=1, source_target_pairs={{0,1},{1,2},{2,3},{4,5},{5,6},{6,7},{8,9},{9,10},{10,11},{12,13},{... | collective-permute-start | bytes 12296 | tf_op jit(solution)/shard_map/ppermute | solution.py:18
  308.9 6.3 collective-permute-start.36
  310.2 5.9 collective-permute-start.37
  316.1 5.8 collective-permute-start.38
  317.4 5.9 collective-permute-start.39
  329.6 6.0 collective-permute-start.42
  330.9 5.9 collective-permute-start.43
  340.2 15.1 %collective-permute-start.44 = (f32[1,128,512]{1,2,0:T(8,128)}, f32[1,128,512]{1,2,0:T(8,128)S(1)}, u32[]{:S(2)}, u32[]{:S(2)}) collective-permute-start(f32[1,128,512]{1,2,0:T(8,128)} %bitcast.14), channel_id=1, source_target_pairs={{4,0},{8,4},{12,8},{16,12},{20,16},{24,20},{28,24},{32,28},{36,32}... | collective-permute-start | bytes 786440 | tf_op jit(solution)/shard_map/ppermute | solution.py:19
  344.9 10.3 %collective-permute-start.45 = (f32[1,128,512]{1,2,0:T(8,128)}, f32[1,128,512]{1,2,0:T(8,128)}, u32[]{:S(2)}, u32[]{:S(2)}) collective-permute-start(f32[1,128,512]{1,2,0:T(8,128)} %bitcast.16), channel_id=1, source_target_pairs={{0,4},{4,8},{8,12},{12,16},{16,20},{20,24},{24,28},{28,32},{32,36}... | collective-permute-start | bytes 786440 | tf_op jit(solution)/shard_map/ppermute | solution.py:18
  362.0 15.5 %collective-permute-start.46 = (f32[6,1,512]{2,1,0:T(1,128)S(1)}, f32[6,1,512]{2,1,0:T(1,128)}, u32[]{:S(2)}, u32[]{:S(2)}) collective-permute-start(f32[6,1,512]{2,1,0:T(1,128)S(1)} %copy.153), channel_id=1, source_target_pairs={{1,0},{2,1},{3,2},{5,4},{6,5},{7,6},{9,8},{10,9},{11,10},{13,12},{... | collective-permute-start | bytes 36872 | tf_op jit(solution)/shard_map/ppermute | solution.py:19
  365.7 14.1 %collective-permute-start.47 = (f32[6,1,512]{2,1,0:T(1,128)}, f32[6,1,512]{2,1,0:T(1,128)}, u32[]{:S(2)}, u32[]{:S(2)}) collective-permute-start(f32[6,1,512]{2,1,0:T(1,128)} %copy.155), channel_id=1, source_target_pairs={{0,1},{1,2},{2,3},{4,5},{5,6},{6,7},{8,9},{9,10},{10,11},{12,13},{... | collective-permute-start | bytes 36872 | tf_op jit(solution)/shard_map/ppermute | solution.py:18
  388.8 6.7 %collective-permute-start.48 = (f32[1,128,512]{1,2,0:T(8,128)S(1)}, f32[1,128,512]{1,2,0:T(8,128)S(1)}, u32[]{:S(2)}, u32[]{:S(2)}) collective-permute-start(f32[1,128,512]{1,2,0:T(8,128)S(1)} %get-tuple-element.33), channel_id=1, source_target_pairs={{4,0},{8,4},{12,8},{16,12},{20,16},{24,20},{28,24},{32,28},{36,32}... | collective-permute-start | bytes 786440 | tf_op jit(solution)/shard_map/ppermute | solution.py:19
  390.1 6.5 collective-permute-start.49
  401.5 7.9 %collective-permute-start.50 = (f32[6,1,512]{2,1,0:T(1,128)S(1)}, f32[6,1,512]{2,1,0:T(1,128)S(1)}, u32[]{:S(2)}, u32[]{:S(2)}) collective-permute-start(f32[6,1,512]{2,1,0:T(1,128)S(1)} %copy.159), channel_id=1, source_target_pairs={{1,0},{2,1},{3,2},{5,4},{6,5},{7,6},{9,8},{10,9},{11,10},{13,12},{... | collective-permute-start | bytes 36872 | tf_op jit(solution)/shard_map/ppermute | solution.py:19
  404.7 6.4 collective-permute-start.51
  418.0 11.1 %collective-permute-start.52 = (f32[1,128,512]{1,2,0:T(8,128)S(1)}, f32[1,128,512]{1,2,0:T(8,128)S(1)}, u32[]{:S(2)}, u32[]{:S(2)}) collective-permute-start(f32[1,128,512]{1,2,0:T(8,128)S(1)} %get-tuple-element.31), channel_id=1, source_target_pairs={{4,0},{8,4},{12,8},{16,12},{20,16},{24,20},{28,24},{32,28},{36,32}... | collective-permute-start | bytes 786440 | tf_op jit(solution)/shard_map/ppermute | solution.py:19
  419.3 10.9 %collective-permute-start.53 = (f32[1,128,512]{1,2,0:T(8,128)S(1)}, f32[1,128,512]{1,2,0:T(8,128)S(1)}, u32[]{:S(2)}, u32[]{:S(2)}) collective-permute-start(f32[1,128,512]{1,2,0:T(8,128)S(1)} %get-tuple-element.30), channel_id=1, source_target_pairs={{0,4},{4,8},{8,12},{12,16},{16,20},{20,24},{24,28},{28,32},{32,36}... | collective-permute-start | bytes 786440 | tf_op jit(solution)/shard_map/ppermute | solution.py:18
  435.0 8.0 %collective-permute-start.54 = (f32[6,1,512]{2,1,0:T(1,128)S(1)}, f32[6,1,512]{2,1,0:T(1,128)S(1)}, u32[]{:S(2)}, u32[]{:S(2)}) collective-permute-start(f32[6,1,512]{2,1,0:T(1,128)S(1)} %copy.165), channel_id=1, source_target_pairs={{1,0},{2,1},{3,2},{5,4},{6,5},{7,6},{9,8},{10,9},{11,10},{13,12},{... | collective-permute-start | bytes 36872 | tf_op jit(solution)/shard_map/ppermute | solution.py:19
  438.2 6.5 collective-permute-start.55
  454.4 174.2 %all-gather.2.cloned.1.call-start = ((), (), s32[]{:S(2)}) async-start(), calls=%async_computation.1 | async-start | bytes 2621440 | tf_op jit(solution)/shard_map/all_gather | solution.py:119
  (47 other events, 654.4 us)
Sparse Core Ops, SparseCore 0:
  454.5 138.3 all-reduce.15
  594.6 33.9 all-gather.1
where the time goes:
time: 680 us; the launch traced here: 669 us
  waiting for transfers between devices  193 us (28%)
  starting transfers between devices  182 us (27%)
  local copies, waits for them, and re-layouts  181 us (27%)
  other arithmetic  97.8 us (14%)
  between operations  15.6 us (2%)
    ppermute x28, starting transfers between devices, with_halo(): before = lax.ppermute(last, axis, up)  146 us
    psum x1, waiting for transfers between devices, shards(): summed_faces = lax.psum(jnp.stack([low_part, high_part]), 'slab')  138 us
    reshape x1, local copies, waits for them, and re-layouts, children_sum(): blocks = field.reshape(x_cells // 2, 2, y_cells // 2, 2, z_cells // 2, 2)  69.2 us
    ppermute x28, starting transfers between devices, with_halo(): after = lax.ppermute(initial, axis, down)  36.1 us
    all_gather x1, waiting for transfers between devices, shards(): all_faces = lax.all_gather(summed_faces, 'pencil', axis=1, tiled=True)  32.8 us
    scatter-add x1, other arithmetic, add_rows(): jax.ops.segment_sum(rows_data, segment_ids, num_segments=slot_count + 1)  29 us
    slice x25, local copies, waits for them, and re-layouts, with_halo(): last = lax.slice_in_dim(x, length - width, length, axis=dim)  27.3 us
    concatenate x28, other arithmetic, with_halo(): x = jnp.concatenate([before, x, after], axis=dim)  26.3 us
  transfers between devices with their start and end apart: 58, of which 22 were waited for; matrix products, arithmetic and copies ran while one was open for 7% of the time, Pallas kernels for 0%

commit v1 on v0

--- a/solution.py
+++ b/solution.py
@@ -115,7 +115,7 @@
     slab_count = lax.axis_size("slab")
     low_part = jnp.where(slab_index == 0, rhs_grad[0], 0.0)
     high_part = jnp.where(slab_index == slab_count - 1, rhs_grad[x_cells - 1], 0.0)
-    summed_faces = lax.psum(jnp.stack([low_part, high_part]), "slab")
+    summed_faces = jnp.sum(lax.all_gather(jnp.stack([low_part, high_part]), "slab"), axis=0)
     all_faces = lax.all_gather(summed_faces, "pencil", axis=1, tiled=True)
     all_rows = tile_rows(all_faces, tile_size)
     targets = source_rows(seg_rows, owners, offsets, tile_size)

time: 680 us -> 656 us (0.965)
  waiting for transfers between devices: 193 us -> 160 us
  other arithmetic: 97.8 us -> 105 us
    psum x1 -> x0, waiting for transfers between devices: 138 us -> none  [shards(): summed_faces = lax.psum(jnp.stack([low_part, high_part]), 'slab')]
    all_gather x0 -> x1, waiting for transfers between devices: none -> 107 us  [shards(): lax.all_gather(jnp.stack([low_part, high_part]), 'slab')]
    reduce_sum x0 -> x1, other arithmetic: none -> 7.84 us  [shards(): jnp.sum(lax.all_gather(jnp.stack([low_part, high_part]), 'slab'), axis=0)]
where the time goes in v1:
time: 656 us; the launch traced here: 645 us
  starting transfers between devices  183 us (28%)
  local copies, waits for them, and re-layouts  182 us (28%)
  waiting for transfers between devices  160 us (24%)
  other arithmetic  105 us (16%)
  between operations  15.6 us (2%)
    ppermute x28, starting transfers between devices, with_halo(): before = lax.ppermute(last, axis, up)  146 us
    all_gather x1, waiting for transfers between devices, shards(): lax.all_gather(jnp.stack([low_part, high_part]), 'slab')  107 us
    reshape x1, local copies, waits for them, and re-layouts, children_sum(): blocks = field.reshape(x_cells // 2, 2, y_cells // 2, 2, z_cells // 2, 2)  69.2 us
    ppermute x28, starting transfers between devices, with_halo(): after = lax.ppermute(initial, axis, down)  36.1 us
    all_gather x1, waiting for transfers between devices, shards(): all_faces = lax.all_gather(summed_faces, 'pencil', axis=1, tiled=True)  32.3 us
    scatter-add x1, other arithmetic, add_rows(): jax.ops.segment_sum(rows_data, segment_ids, num_segments=slot_count + 1)  29 us
    slice x25, local copies, waits for them, and re-layouts, with_halo(): last = lax.slice_in_dim(x, length - width, length, axis=dim)  27.3 us
    concatenate x28, other arithmetic, with_halo(): x = jnp.concatenate([before, x, after], axis=dim)  26.3 us
  transfers between devices with their start and end apart: 58, of which 22 were waited for; matrix products, arithmetic and copies ran while one was open for 7% of the time, Pallas kernels for 0%

profile of v1, /device:TPU:0, one launch (start us, length us, event | category | flops | bytes accessed | tf_op | source)
XLA Modules:
  0.0 644.9 jit_solution(2014478268066024557)
XLA Ops:
  10.1 3.0 collective-permute-start.1
  21.6 4.6 collective-permute-start.3
  29.2 3.6 select_maximum_fusion.20
  32.8 2.7 fusion.29
  36.8 5.0 collective-permute-start.5
  50.3 4.5 collective-permute-start.7
  58.2 3.3 select_maximum_fusion.16
  61.6 2.4 fusion.24
  65.4 8.1 %collective-permute-start.9 = (f32[1,128,512]{1,2,0:T(8,128)S(1)}, f32[1,128,512]{1,2,0:T(8,128)S(1)}, u32[]{:S(2)}, u32[]{:S(2)}) collective-permute-start(f32[1,128,512]{1,2,0:T(8,128)S(1)} %get-tuple-element.34), channel_id=1, source_target_pairs={{0,4},{4,8},{8,12},{12,16},{16,20},{20,24},{24,28},{28,32},{32,36}... | collective-permute-start | bytes 786440 | tf_op jit(solution)/shard_map/ppermute | solution.py:18
  82.6 5.1 collective-permute-start.11
  91.1 3.3 select_maximum_fusion.12
  94.5 2.4 fusion.19
  96.9 2.6 copy.139
  99.4 69.2 %reshape.120 = f32[2,2,64,2,256,2]{5,4,3,2,1,0:T(8,128)} reshape(f32[4,128,512]{2,1,0:T(8,128)} %copy.139) | data formatting | bytes 2097152 | tf_op jit(solution)/shard_map/reshape | solution.py:51
  168.6 20.8 %reduce_sum.45 = f32[2,64,256]{2,1,0:T(8,128)S(1)} reduce(f32[2,2,64,2,256,2]{5,4,3,2,1,0:T(8,128)} %reshape.120, f32[]{:T(128)} %constant.17.clone.1), dimensions={1,3,5}, to_apply=%region_0.1 | reduce | flops 229376 | bytes 1179652 | tf_op jit(solution)/shard_map/reduce_sum | solution.py:52
  190.7 7.2 %collective-permute-start.13 = (f32[1,64,256]{2,1,0:T(8,128)S(1)}, f32[1,64,256]{2,1,0:T(8,128)S(1)}, u32[]{:S(2)}, u32[]{:S(2)}) collective-permute-start(f32[1,64,256]{2,1,0:T(8,128)S(1)} %get-tuple-element.62), channel_id=1, source_target_pairs={{0,4},{4,8},{8,12},{12,16},{16,20},{20,24},{24,28},{28,32},{32,36}... | collective-permute-start | bytes 196616 | tf_op jit(solution)/shard_map/ppermute | solution.py:18
  200.1 4.5 collective-permute-start.15
  207.6 4.9 collective-permute-start.17
  214.6 4.5 collective-permute-start.19
  222.1 5.6 collective-permute-start.21
  229.9 4.5 collective-permute-start.23
  237.4 6.3 reduce_sum.47
  243.7 2.8 reduce_sum.48
  247.8 5.6 collective-permute-start.25
  255.5 4.5 collective-permute-start.27
  262.8 5.2 collective-permute-start.29
  270.2 4.5 collective-permute-start.31
  281.7 5.8 collective-permute-start.33
  295.9 4.5 collective-permute-start.35
  310.3 5.0 collective-permute-start.37
  317.5 4.6 collective-permute-start.39
  325.0 3.8 collective-permute-start.41
  331.0 4.7 collective-permute-start.43
  345.1 6.3 collective-permute-start.45
  363.4 2.5 copy.156
  365.9 5.1 collective-permute-start.47
  382.5 3.7 select_maximum_fusion.8
  386.6 2.4 fusion.14
  390.3 5.4 collective-permute-start.49
  404.8 4.8 collective-permute-start.51
  413.0 3.7 select_maximum_fusion.4
  419.5 9.8 %collective-permute-start.53 = (f32[1,128,512]{1,2,0:T(8,128)S(1)}, f32[1,128,512]{1,2,0:T(8,128)S(1)}, u32[]{:S(2)}, u32[]{:S(2)}) collective-permute-start(f32[1,128,512]{1,2,0:T(8,128)S(1)} %get-tuple-element.30), channel_id=1, source_target_pairs={{0,4},{4,8},{8,12},{12,16},{16,20},{20,24},{24,28},{28,32},{32,36}... | collective-permute-start | bytes 786440 | tf_op jit(solution)/shard_map/ppermute | solution.py:18
  438.4 4.8 collective-permute-start.55
  446.6 3.7 select_maximum_fusion
  455.0 106.6 %all-gather.6.cloned.1.call-done = f32[64,128,512]{2,1,0:T(8,128)} async-done(((f32[2,128,512]{2,1,0:T(8,128)}), f32[64,128,512]{2,1,0:T(8,128)}) %all-gather.6.cloned.1.call-update) | async-done | bytes 16777232 | tf_op jit(solution)/shard_map/all_gather | solution.py:118
  561.7 7.8 %reduce_sum.51 = f32[2,128,512]{2,1,0:T(8,128)S(1)} reduce(f32[32,2,128,512]{3,2,1,0:T(8,128)} %bitcast.39, f32[]{:T(128)} %constant.17.clone.1), dimensions={0}, to_apply=%region_5.6 | reduce | flops 4063232 | bytes 17301508 | tf_op jit(solution)/shard_map/reduce_sum | solution.py:118
  572.1 32.3 %all-gather.4.cloned.1.call-done = f32[2,512,512]{1,2,0:T(8,128)} async-done(((f32[2,128,512]{1,2,0:T(8,128)}), f32[2,512,512]{1,2,0:T(8,128)}) %all-gather.4.cloned.1.call-update) | async-done | bytes 2097168 | tf_op jit(solution)/shard_map/all_gather | solution.py:119
  608.2 29.0 %scatter_custom_fusion = f32[129,128]{1,0:T(8,128)S(1)} fusion(s32[4096]{0:T(1024)S(1)} %bitcast.56, f32[4096,128]{1,0:T(8,128)} %bitcast.42, f32[]{:T(128)} %constant.17.clone.1), kind=kCustom, calls=%fused_computation.276 | custom fusion | flops 524288 | bytes 66560 | tf_op jit(solution)/shard_map/scatter-add | solution.py:78
  (283 shorter events, 172.1 us)
Async XLA Ops:
  7.2 554.5 %all-gather.6.cloned.1.call-start = ((), (), s32[]{:S(2)}) async-start(), calls=%async_computation.1 | async-start | bytes 17301504 | tf_op jit(solution)/shard_map/all_gather | solution.py:118
  18.4 7.7 %collective-permute-start.2 = (f32[6,1,512]{2,1,0:T(1,128)S(1)}, f32[6,1,512]{2,1,0:T(1,128)S(1)}, u32[]{:S(2)}, u32[]{:S(2)}) collective-permute-start(f32[6,1,512]{2,1,0:T(1,128)S(1)} %copy.120), channel_id=1, source_target_pairs={{1,0},{2,1},{3,2},{5,4},{6,5},{7,6},{9,8},{10,9},{11,10},{13,12},{... | collective-permute-start | bytes 36872 | tf_op jit(solution)/shard_map/ppermute | solution.py:19
  21.6 6.0 collective-permute-start.3
  35.5 6.4 collective-permute-start.4
  36.8 6.2 collective-permute-start.5
  47.2 7.7 %collective-permute-start.6 = (f32[6,1,512]{2,1,0:T(1,128)S(1)}, f32[6,1,512]{2,1,0:T(1,128)S(1)}, u32[]{:S(2)}, u32[]{:S(2)}) collective-permute-start(f32[6,1,512]{2,1,0:T(1,128)S(1)} %copy.127), channel_id=1, source_target_pairs={{1,0},{2,1},{3,2},{5,4},{6,5},{7,6},{9,8},{10,9},{11,10},{13,12},{... | collective-permute-start | bytes 36872 | tf_op jit(solution)/shard_map/ppermute | solution.py:19
  50.3 6.2 collective-permute-start.7
  64.1 9.4 %collective-permute-start.8 = (f32[1,128,512]{1,2,0:T(8,128)S(1)}, f32[1,128,512]{1,2,0:T(8,128)S(1)}, u32[]{:S(2)}, u32[]{:S(2)}) collective-permute-start(f32[1,128,512]{1,2,0:T(8,128)S(1)} %get-tuple-element.35), channel_id=1, source_target_pairs={{4,0},{8,4},{12,8},{16,12},{20,16},{24,20},{28,24},{32,28},{36,32}... | collective-permute-start | bytes 786440 | tf_op jit(solution)/shard_map/ppermute | solution.py:19
  65.4 9.3 %collective-permute-start.9 = (f32[1,128,512]{1,2,0:T(8,128)S(1)}, f32[1,128,512]{1,2,0:T(8,128)S(1)}, u32[]{:S(2)}, u32[]{:S(2)}) collective-permute-start(f32[1,128,512]{1,2,0:T(8,128)S(1)} %get-tuple-element.34), channel_id=1, source_target_pairs={{0,4},{4,8},{8,12},{12,16},{16,20},{20,24},{24,28},{28,32},{32,36}... | collective-permute-start | bytes 786440 | tf_op jit(solution)/shard_map/ppermute | solution.py:18
  79.5 8.3 %collective-permute-start.10 = (f32[6,1,512]{2,1,0:T(1,128)S(1)}, f32[6,1,512]{2,1,0:T(1,128)S(1)}, u32[]{:S(2)}, u32[]{:S(2)}) collective-permute-start(f32[6,1,512]{2,1,0:T(1,128)S(1)} %copy.133), channel_id=1, source_target_pairs={{1,0},{2,1},{3,2},{5,4},{6,5},{7,6},{9,8},{10,9},{11,10},{13,12},{... | collective-permute-start | bytes 36872 | tf_op jit(solution)/shard_map/ppermute | solution.py:19
  82.6 6.8 %collective-permute-start.11 = (f32[6,1,512]{2,1,0:T(1,128)S(1)}, f32[6,1,512]{2,1,0:T(1,128)S(1)}, u32[]{:S(2)}, u32[]{:S(2)}) collective-permute-start(f32[6,1,512]{2,1,0:T(1,128)S(1)} %copy.135), channel_id=1, source_target_pairs={{0,1},{1,2},{2,3},{4,5},{5,6},{6,7},{8,9},{9,10},{10,11},{12,13},{... | collective-permute-start | bytes 36872 | tf_op jit(solution)/shard_map/ppermute | solution.py:18
  189.4 8.5 %collective-permute-start.12 = (f32[1,64,256]{2,1,0:T(8,128)S(1)}, f32[1,64,256]{2,1,0:T(8,128)S(1)}, u32[]{:S(2)}, u32[]{:S(2)}) collective-permute-start(f32[1,64,256]{2,1,0:T(8,128)S(1)} %get-tuple-element.63), channel_id=1, source_target_pairs={{4,0},{8,4},{12,8},{16,12},{20,16},{24,20},{28,24},{32,28},{36,32}... | collective-permute-start | bytes 196616 | tf_op jit(solution)/shard_map/ppermute | solution.py:19
  190.7 8.1 %collective-permute-start.13 = (f32[1,64,256]{2,1,0:T(8,128)S(1)}, f32[1,64,256]{2,1,0:T(8,128)S(1)}, u32[]{:S(2)}, u32[]{:S(2)}) collective-permute-start(f32[1,64,256]{2,1,0:T(8,128)S(1)} %get-tuple-element.62), channel_id=1, source_target_pairs={{0,4},{4,8},{8,12},{12,16},{16,20},{20,24},{24,28},{28,32},{32,36}... | collective-permute-start | bytes 196616 | tf_op jit(solution)/shard_map/ppermute | solution.py:18
  198.8 5.8 collective-permute-start.14
  200.1 5.9 collective-permute-start.15
  206.3 6.2 collective-permute-start.16
  214.6 5.9 collective-permute-start.19
  220.8 6.9 %collective-permute-start.20 = (f32[1,64,256]{2,1,0:T(8,128)S(1)}, f32[1,64,256]{2,1,0:T(8,128)S(1)}, u32[]{:S(2)}, u32[]{:S(2)}) collective-permute-start(f32[1,64,256]{2,1,0:T(8,128)S(1)} %get-tuple-element.59), channel_id=1, source_target_pairs={{4,0},{8,4},{12,8},{16,12},{20,16},{24,20},{28,24},{32,28},{36,32}... | collective-permute-start | bytes 196616 | tf_op jit(solution)/shard_map/ppermute | solution.py:19
  222.1 6.5 %collective-permute-start.21 = (f32[1,64,256]{2,1,0:T(8,128)S(1)}, f32[1,64,256]{2,1,0:T(8,128)S(1)}, u32[]{:S(2)}, u32[]{:S(2)}) collective-permute-start(f32[1,64,256]{2,1,0:T(8,128)S(1)} %get-tuple-element.58), channel_id=1, source_target_pairs={{0,4},{4,8},{8,12},{12,16},{16,20},{20,24},{24,28},{28,32},{32,36}... | collective-permute-start | bytes 196616 | tf_op jit(solution)/shard_map/ppermute | solution.py:18
  228.6 5.8 collective-permute-start.22
  229.9 5.9 collective-permute-start.23
  246.5 6.9 %collective-permute-start.24 = (f32[1,32,128]{2,1,0:T(8,128)S(1)}, f32[1,32,128]{2,1,0:T(8,128)S(1)}, u32[]{:S(2)}, u32[]{:S(2)}) collective-permute-start(f32[1,32,128]{2,1,0:T(8,128)S(1)} %bitcast.48), channel_id=1, source_target_pairs={{4,0},{8,4},{12,8},{16,12},{20,16},{24,20},{28,24},{32,28},{36,32}... | collective-permute-start | bytes 49160 | tf_op jit(solution)/shard_map/ppermute | solution.py:19
  247.8 6.4 collective-permute-start.25
  261.6 6.5 %collective-permute-start.28 = (f32[1,32,128]{2,1,0:T(8,128)S(1)}, f32[1,32,128]{2,1,0:T(8,128)S(1)}, u32[]{:S(2)}, u32[]{:S(2)}) collective-permute-start(f32[1,32,128]{2,1,0:T(8,128)S(1)} %fusion.81), channel_id=1, source_target_pairs={{4,0},{8,4},{12,8},{16,12},{20,16},{24,20},{28,24},{32,28},{36,32}... | collective-permute-start | bytes 49160 | tf_op jit(solution)/shard_map/ppermute | solution.py:19
  262.8 6.0 collective-permute-start.29
  280.5 8.7 %collective-permute-start.32 = (f32[1,64,256]{1,2,0:T(8,128)}, f32[1,64,256]{1,2,0:T(8,128)}, u32[]{:S(2)}, u32[]{:S(2)}) collective-permute-start(f32[1,64,256]{1,2,0:T(8,128)} %bitcast.7), channel_id=1, source_target_pairs={{4,0},{8,4},{12,8},{16,12},{20,16},{24,20},{28,24},{32,28},{36,32}... | collective-permute-start | bytes 196616 | tf_op jit(solution)/shard_map/ppermute | solution.py:19
  281.7 9.0 %collective-permute-start.33 = (f32[1,64,256]{1,2,0:T(8,128)}, f32[1,64,256]{1,2,0:T(8,128)}, u32[]{:S(2)}, u32[]{:S(2)}) collective-permute-start(f32[1,64,256]{1,2,0:T(8,128)} %bitcast.7), channel_id=1, source_target_pairs={{0,4},{4,8},{8,12},{12,16},{16,20},{20,24},{24,28},{28,32},{32,36}... | collective-permute-start | bytes 196616 | tf_op jit(solution)/shard_map/ppermute | solution.py:18
  294.6 11.9 %collective-permute-start.34 = (f32[4,1,256]{2,1,0:T(1,128)S(1)}, f32[4,1,256]{2,1,0:T(1,128)S(1)}, u32[]{:S(2)}, u32[]{:S(2)}) collective-permute-start(f32[4,1,256]{2,1,0:T(1,128)S(1)} %get-tuple-element.47), channel_id=1, source_target_pairs={{1,0},{2,1},{3,2},{5,4},{6,5},{7,6},{9,8},{10,9},{11,10},{13,12},{... | collective-permute-start | bytes 12296 | tf_op jit(solution)/shard_map/ppermute | solution.py:19
  295.9 10.6 %collective-permute-start.35 = (f32[4,1,256]{2,1,0:T(1,128)S(1)}, f32[4,1,256]{2,1,0:T(1,128)S(1)}, u32[]{:S(2)}, u32[]{:S(2)}) collective-permute-start(f32[4,1,256]{2,1,0:T(1,128)S(1)} %get-tuple-element.46), channel_id=1, source_target_pairs={{0,1},{1,2},{2,3},{4,5},{5,6},{6,7},{8,9},{9,10},{10,11},{12,13},{... | collective-permute-start | bytes 12296 | tf_op jit(solution)/shard_map/ppermute | solution.py:18
  309.0 6.3 collective-permute-start.36
  310.3 5.9 collective-permute-start.37
  316.2 5.8 collective-permute-start.38
  317.5 5.9 collective-permute-start.39
  329.7 6.0 collective-permute-start.42
  331.0 5.9 collective-permute-start.43
  340.3 15.1 %collective-permute-start.44 = (f32[1,128,512]{1,2,0:T(8,128)}, f32[1,128,512]{1,2,0:T(8,128)S(1)}, u32[]{:S(2)}, u32[]{:S(2)}) collective-permute-start(f32[1,128,512]{1,2,0:T(8,128)} %bitcast.14), channel_id=1, source_target_pairs={{4,0},{8,4},{12,8},{16,12},{20,16},{24,20},{28,24},{32,28},{36,32}... | collective-permute-start | bytes 786440 | tf_op jit(solution)/shard_map/ppermute | solution.py:19
  345.1 10.4 %collective-permute-start.45 = (f32[1,128,512]{1,2,0:T(8,128)}, f32[1,128,512]{1,2,0:T(8,128)}, u32[]{:S(2)}, u32[]{:S(2)}) collective-permute-start(f32[1,128,512]{1,2,0:T(8,128)} %bitcast.16), channel_id=1, source_target_pairs={{0,4},{4,8},{8,12},{12,16},{16,20},{20,24},{24,28},{28,32},{32,36}... | collective-permute-start | bytes 786440 | tf_op jit(solution)/shard_map/ppermute | solution.py:18
  362.1 15.6 %collective-permute-start.46 = (f32[6,1,512]{2,1,0:T(1,128)S(1)}, f32[6,1,512]{2,1,0:T(1,128)}, u32[]{:S(2)}, u32[]{:S(2)}) collective-permute-start(f32[6,1,512]{2,1,0:T(1,128)S(1)} %copy.154), channel_id=1, source_target_pairs={{1,0},{2,1},{3,2},{5,4},{6,5},{7,6},{9,8},{10,9},{11,10},{13,12},{... | collective-permute-start | bytes 36872 | tf_op jit(solution)/shard_map/ppermute | solution.py:19
  365.9 14.2 %collective-permute-start.47 = (f32[6,1,512]{2,1,0:T(1,128)}, f32[6,1,512]{2,1,0:T(1,128)}, u32[]{:S(2)}, u32[]{:S(2)}) collective-permute-start(f32[6,1,512]{2,1,0:T(1,128)} %copy.156), channel_id=1, source_target_pairs={{0,1},{1,2},{2,3},{4,5},{5,6},{6,7},{8,9},{9,10},{10,11},{12,13},{... | collective-permute-start | bytes 36872 | tf_op jit(solution)/shard_map/ppermute | solution.py:18
  389.0 6.7 %collective-permute-start.48 = (f32[1,128,512]{1,2,0:T(8,128)S(1)}, f32[1,128,512]{1,2,0:T(8,128)S(1)}, u32[]{:S(2)}, u32[]{:S(2)}) collective-permute-start(f32[1,128,512]{1,2,0:T(8,128)S(1)} %get-tuple-element.33), channel_id=1, source_target_pairs={{4,0},{8,4},{12,8},{16,12},{20,16},{24,20},{28,24},{32,28},{36,32}... | collective-permute-start | bytes 786440 | tf_op jit(solution)/shard_map/ppermute | solution.py:19
  390.3 6.5 %collective-permute-start.49 = (f32[1,128,512]{1,2,0:T(8,128)S(1)}, f32[1,128,512]{1,2,0:T(8,128)S(1)}, u32[]{:S(2)}, u32[]{:S(2)}) collective-permute-start(f32[1,128,512]{1,2,0:T(8,128)S(1)} %get-tuple-element.32), channel_id=1, source_target_pairs={{0,4},{4,8},{8,12},{12,16},{16,20},{20,24},{24,28},{28,32},{32,36}... | collective-permute-start | bytes 786440 | tf_op jit(solution)/shard_map/ppermute | solution.py:18
  401.7 7.9 %collective-permute-start.50 = (f32[6,1,512]{2,1,0:T(1,128)S(1)}, f32[6,1,512]{2,1,0:T(1,128)S(1)}, u32[]{:S(2)}, u32[]{:S(2)}) collective-permute-start(f32[6,1,512]{2,1,0:T(1,128)S(1)} %copy.160), channel_id=1, source_target_pairs={{1,0},{2,1},{3,2},{5,4},{6,5},{7,6},{9,8},{10,9},{11,10},{13,12},{... | collective-permute-start | bytes 36872 | tf_op jit(solution)/shard_map/ppermute | solution.py:19
  404.8 6.4 collective-permute-start.51
  418.2 11.1 %collective-permute-start.52 = (f32[1,128,512]{1,2,0:T(8,128)S(1)}, f32[1,128,512]{1,2,0:T(8,128)S(1)}, u32[]{:S(2)}, u32[]{:S(2)}) collective-permute-start(f32[1,128,512]{1,2,0:T(8,128)S(1)} %get-tuple-element.31), channel_id=1, source_target_pairs={{4,0},{8,4},{12,8},{16,12},{20,16},{24,20},{28,24},{32,28},{36,32}... | collective-permute-start | bytes 786440 | tf_op jit(solution)/shard_map/ppermute | solution.py:19
  419.5 10.9 %collective-permute-start.53 = (f32[1,128,512]{1,2,0:T(8,128)S(1)}, f32[1,128,512]{1,2,0:T(8,128)S(1)}, u32[]{:S(2)}, u32[]{:S(2)}) collective-permute-start(f32[1,128,512]{1,2,0:T(8,128)S(1)} %get-tuple-element.30), channel_id=1, source_target_pairs={{0,4},{4,8},{8,12},{12,16},{16,20},{20,24},{24,28},{28,32},{32,36}... | collective-permute-start | bytes 786440 | tf_op jit(solution)/shard_map/ppermute | solution.py:18
  435.2 8.0 %collective-permute-start.54 = (f32[6,1,512]{2,1,0:T(1,128)S(1)}, f32[6,1,512]{2,1,0:T(1,128)S(1)}, u32[]{:S(2)}, u32[]{:S(2)}) collective-permute-start(f32[6,1,512]{2,1,0:T(1,128)S(1)} %copy.166), channel_id=1, source_target_pairs={{1,0},{2,1},{3,2},{5,4},{6,5},{7,6},{9,8},{10,9},{11,10},{13,12},{... | collective-permute-start | bytes 36872 | tf_op jit(solution)/shard_map/ppermute | solution.py:19
  438.4 6.5 %collective-permute-start.55 = (f32[6,1,512]{2,1,0:T(1,128)S(1)}, f32[6,1,512]{2,1,0:T(1,128)S(1)}, u32[]{:S(2)}, u32[]{:S(2)}) collective-permute-start(f32[6,1,512]{2,1,0:T(1,128)S(1)} %copy.168), channel_id=1, source_target_pairs={{0,1},{1,2},{2,3},{4,5},{5,6},{6,7},{8,9},{9,10},{10,11},{12,13},{... | collective-permute-start | bytes 36872 | tf_op jit(solution)/shard_map/ppermute | solution.py:18
  454.7 149.7 %all-gather.4.cloned.1.call-start = ((), (), s32[]{:S(2)}) async-start(), calls=%async_computation | async-start | bytes 2621440 | tf_op jit(solution)/shard_map/all_gather | solution.py:119
  (48 other events, 262.9 us)
Sparse Core Ops, SparseCore 0:
  454.9 106.7 all-gather.5
  570.7 33.6 all-gather.3
